TPU v7x, 128 devices: a whole 4x4x4 slice. The times are simulated.
128 devices in a mesh: req: 16 (over z, y), exp: 8 (over x, core).
Axes of the slice: x: 4, y: 4, z: 4, core: 2. Of those that a mesh axis runs over, the one named last changes fastest.
Arguments:
- residual: bfloat16 [16384, 2048], P(('req', 'exp')), may hold values from -3 to 3
- query_vectors: bfloat16 [16384, 2048], P(('req', 'exp')), may hold values from -12 to 12
- key_vectors: bfloat16 [16384, 2048], P(('req', 'exp')), may hold values from -12 to 12
- value_vectors: bfloat16 [16384, 2048], P(('req', 'exp')), may hold values from -6 to 6
- segment_ids: int32 [16384], P('req'), may hold values from 0 to 2, as said below
- prompt_lengths: int32 [16, 3], replicated, may hold values from 1 to 512, as said below
- request_groups: int32 [16], replicated, may hold values from 0 to 15, as said below
- page_table: int32 [16, 8], replicated, may hold values from 0 to 127, as said below
- expert_ids: int32 [16384, 8], P(('req', 'exp')), may hold values from 0 to 63, all different within a row; in each aligned block of 128 rows (0 to 127, 128 to 255, ...) at most 24 rows name the same one
- gate_weights: float32 [16384, 8], P(('req', 'exp')), may hold values from 0.1 to 0.6
- out_weight: bfloat16 [2048, 2048], replicated, may hold values from -0.125 to 0.125
- norm_gain: float32 [2048], replicated, may hold values from 0.5 to 2
- expert_inner: bfloat16 [128, 2048, 1024], P(('req', 'exp')), may hold values from -0.125 to 0.125
- expert_outer: bfloat16 [128, 512, 2048], P(('req', 'exp')), may hold values from -0.1875 to 0.1875
Outputs:
- layer_out: bfloat16 [16384, 2048], P(('req', 'exp'))
- kv_pages: bfloat16 [128, 2, 128, 2048], P('req', None, None, 'exp')
Inputs may be any that keep to these rules, and one draw needn't show every extreme that they name: `prompt_lengths`: each row sums to 1024, and its largest entry is 512. `segment_ids`: within each group of 1024 rows the numbers never fall; prompt j of the request r with request_groups[r] = g fills prompt_lengths[r, j] consecutive rows of group g. `request_groups`: each group appears once. `page_table`: all entries differ; the 8 pages of one request lie in 8 different owner groups, the owner of slot s being s // 8. `expert_ids`: the 8 ids of a token differ; among the 128 tokens of one device no expert is named more than 24 times, a bound that some block reaches.
All inputs are finite; a program needn't handle non-finite values.
Results may differ from a plain program's by a relative error of at most 0.013.
Values may be sent and summed in bfloat16 or wider, within the bound.
No kernel may reach another device: no remote copies, remote signals or barrier semaphores. Data moves between devices by JAX's collectives and lax.ppermute only.
A program may use at most 192 MiB of HBM per device.

v0:
```python
import jax
import jax.numpy as jnp
from jax import lax
from jax.sharding import PartitionSpec as P

HEAD = 128
PAGE = 128


rope_base = 10000.0
norm_eps = 1e-06
masked_score = -1e30


def partner(value, axis, distance):
    return lax.ppermute(value, axis, [(i, i ^ 1 << distance) for i in range(lax.axis_size(axis))])


def rotate(values_in, positions):
    row_count = values_in.shape[0]
    half_head = HEAD // 2
    inverse = rope_base ** (-(2.0 * jnp.arange(half_head, dtype=jnp.float32)) / HEAD)
    angles = positions[:, None] * inverse[None, :]
    cosine = jnp.cos(angles)[:, None, :]
    sines = jnp.sin(angles)[:, None, :]
    shaped = values_in.astype(jnp.float32).reshape(row_count, -1, HEAD)
    first_half = shaped[..., :half_head]
    second_half = shaped[..., half_head:]
    turned = jnp.concatenate(
        [first_half * cosine - second_half * sines, second_half * cosine + first_half * sines],
        axis=-1,
    )
    return turned.reshape(row_count, -1).astype(jnp.bfloat16)


def score_block(query_block, query_segments, key_block, key_segments):
    scores = jnp.einsum(
        "qhd,khd->hqk", query_block, key_block, preferred_element_type=jnp.float32
    ) * HEAD ** (-0.5)
    same_prompt = (query_segments[:, None] == key_segments[None, :])[None]
    return (jnp.where(same_prompt, scores, masked_score), same_prompt)


def attend_all(query_heads, key_heads, value_heads, group_segments, block_rows):
    block_count = query_heads.shape[0] // block_rows

    def one_block(block_index):
        start_row = block_index * block_rows
        query_block = lax.dynamic_slice_in_dim(query_heads, start_row, block_rows, 0)
        query_segments = lax.dynamic_slice_in_dim(group_segments, start_row, block_rows, 0)
        scores, same_prompt = score_block(query_block, query_segments, key_heads, group_segments)
        top_score = jnp.max(scores, axis=-1, keepdims=True)
        weights = jnp.where(same_prompt, jnp.exp(scores - top_score), 0.0)
        totals = jnp.sum(weights, axis=-1)
        mixed = jnp.einsum(
            "hqk,khd->qhd",
            weights.astype(jnp.bfloat16),
            value_heads,
            preferred_element_type=jnp.float32,
        )
        return (mixed / totals.T[:, :, None]).astype(jnp.bfloat16)

    results = lax.map(one_block, jnp.arange(block_count))
    return results.reshape(query_heads.shape[0], -1)


def send_rows(blocks):
    arrived = lax.all_to_all(blocks, ("req", "exp"), split_axis=0, concat_axis=0, tiled=True)
    return arrived


def send_back(blocks):
    arrived = lax.all_to_all(blocks, ("req", "exp"), split_axis=0, concat_axis=0, tiled=True)
    return arrived


def half_expert(rows, inner_half, outer_half):
    projected = jnp.dot(rows, inner_half, preferred_element_type=jnp.float32)
    half_units = projected.shape[1] // 2
    active = (jax.nn.silu(projected[:, :half_units]) * projected[:, half_units:]).astype(
        jnp.bfloat16
    )
    return jnp.dot(active, outer_half, preferred_element_type=jnp.float32)


def on_device(
    residual,
    query_vectors,
    key_vectors,
    value_vectors,
    segment_ids,
    prompt_lengths,
    request_groups,
    page_table,
    expert_ids,
    gate_weights,
    out_weight,
    norm_gain,
    expert_inner,
    expert_outer,
):
    tok_rows, model_width = residual.shape
    req_count = lax.axis_size("req")
    member_count = lax.axis_size("exp")
    device_count = req_count * member_count
    expert_count = device_count // 2
    group_rows = tok_rows * member_count
    top_count = expert_ids.shape[1]
    capacity = 3 * tok_rows * top_count // (2 * expert_count)
    half_capacity = capacity // 2
    page_count = group_rows // PAGE
    group = lax.axis_index("req")
    member = lax.axis_index("exp")
    parity = member % 2
    holds_request = (request_groups == group).astype(jnp.int32)
    my_lengths = jnp.sum(holds_request[:, None] * prompt_lengths, axis=0)
    my_pages = jnp.sum(holds_request[:, None] * page_table, axis=0)
    starts = jnp.cumsum(my_lengths) - my_lengths
    first_row = member * tok_rows
    my_segments = lax.dynamic_slice_in_dim(segment_ids, first_row, tok_rows, 0)
    prompt_index = jnp.arange(prompt_lengths.shape[1], dtype=jnp.int32)
    token_start = jnp.sum(
        jnp.where(my_segments[:, None] == prompt_index[None, :], starts[None, :], 0), axis=1
    )
    positions = (first_row + jnp.arange(tok_rows, dtype=jnp.int32) - token_start).astype(
        jnp.float32
    )
    query_turned = rotate(query_vectors, positions)
    key_turned = rotate(key_vectors, positions)
    query_group, key_group, value_group = (
        lax.all_to_all(query_turned, "exp", split_axis=1, concat_axis=0, tiled=True),
        lax.all_to_all(key_turned, "exp", split_axis=1, concat_axis=0, tiled=True),
        lax.all_to_all(value_vectors, "exp", split_axis=1, concat_axis=0, tiled=True),
    )
    column_count = key_group.shape[1]
    stacked = jnp.stack(
        [
            key_group.reshape(page_count, PAGE, column_count),
            value_group.reshape(page_count, PAGE, column_count),
        ],
        axis=1,
    ).reshape(page_count, -1)
    owner_of_page = my_pages // page_count
    group_range = jnp.arange(req_count, dtype=jnp.int32)
    send_select = (owner_of_page[None, :] == group_range[:, None]).astype(jnp.bfloat16)
    outgoing_pages = jnp.dot(send_select, stacked, preferred_element_type=jnp.float32).astype(
        jnp.bfloat16
    )
    incoming_pages = lax.all_to_all(outgoing_pages, "req", split_axis=0, concat_axis=0, tiled=True)
    source_holds = (request_groups[None, :] == group_range[:, None]).astype(jnp.int32)
    source_pages = jnp.sum(source_holds[:, :, None] * page_table[None, :, :], axis=1)
    slot_ids = group * page_count + jnp.arange(page_count, dtype=jnp.int32)
    place_select = jnp.sum(
        (source_pages[None, :, :] == slot_ids[:, None, None]).astype(jnp.int32), axis=2
    ).astype(jnp.bfloat16)
    kv_pages = (
        jnp.dot(place_select, incoming_pages, preferred_element_type=jnp.float32)
        .astype(jnp.bfloat16)
        .reshape(page_count, 2, PAGE, column_count)
    )
    heads_here = column_count // HEAD
    query_heads = query_group.reshape(group_rows, heads_here, HEAD)
    key_heads = key_group.reshape(group_rows, heads_here, HEAD)
    value_heads = value_group.reshape(group_rows, heads_here, HEAD)
    block_rows = min(512, group_rows)
    attended = attend_all(query_heads, key_heads, value_heads, segment_ids, block_rows)
    token_heads = lax.all_to_all(attended, "exp", split_axis=0, concat_axis=1, tiled=True)
    hidden = residual.astype(jnp.float32) + jnp.dot(
        token_heads, out_weight, preferred_element_type=jnp.float32
    )
    normed = (
        hidden * lax.rsqrt(jnp.mean(hidden * hidden, axis=-1, keepdims=True) + norm_eps) * norm_gain
    ).astype(jnp.bfloat16)
    expert_range = jnp.arange(expert_count, dtype=jnp.int32)
    chosen = (expert_ids[:, :, None] == expert_range[None, None, :]).astype(jnp.int32)
    picked = jnp.sum(chosen, axis=1)
    earlier = jnp.cumsum(picked, axis=0) - picked
    slot_rank = jnp.sum(chosen * earlier[:, None, :], axis=2)
    slot_index = expert_ids * capacity + slot_rank
    slot_range = jnp.arange(expert_count * capacity, dtype=jnp.int32)
    dispatch_matrix = jnp.sum(
        (slot_index[None, :, :] == slot_range[:, None, None]).astype(jnp.int32), axis=2
    ).astype(jnp.bfloat16)
    packed = (
        jnp.dot(dispatch_matrix, normed, preferred_element_type=jnp.float32)
        .astype(jnp.bfloat16)
        .reshape(expert_count, capacity, model_width)
    )
    doubled = jnp.broadcast_to(packed[:, None], (expert_count, 2, capacity, model_width)).reshape(
        device_count, capacity, model_width
    )
    expert_input = send_rows(doubled)
    flat_input = expert_input.reshape(device_count * capacity, model_width)
    partial_out = half_expert(flat_input, expert_inner[0], expert_outer[0]).reshape(
        device_count, capacity, model_width
    )
    kept = lax.dynamic_slice_in_dim(partial_out, parity * half_capacity, half_capacity, 1)
    handed = lax.dynamic_slice_in_dim(partial_out, (1 - parity) * half_capacity, half_capacity, 1)
    received = partner(handed.astype(jnp.bfloat16), "exp", 0).astype(handed.dtype)
    expert_out = (kept + received).astype(jnp.bfloat16)
    returned = send_back(expert_out).reshape(expert_count * capacity, model_width)
    gathered = returned[slot_index]
    mixed = jnp.einsum("tk,tkd->td", gate_weights, gathered.astype(jnp.float32))
    layer_out = (hidden + mixed).astype(jnp.bfloat16)
    return (layer_out, kv_pages)


def solution(mesh):
    placed = (
        P(("req", "exp"), None),
        P(("req", "exp"), None),
        P(("req", "exp"), None),
        P(("req", "exp"), None),
        P("req"),
        P(),
        P(),
        P(),
        P(("req", "exp"), None),
        P(("req", "exp"), None),
        P(),
        P(),
        P(("req", "exp"), None, None),
        P(("req", "exp"), None, None),
    )
    return jax.shard_map(
        on_device,
        mesh=mesh,
        in_specs=placed,
        out_specs=(P(("req", "exp"), None), P("req", None, None, "exp")),
        check_vma=False,
    )
```

profile of v0, /device:TPU:2, one launch (start us, length us, event | category | flops | bytes accessed | tf_op | source)
XLA Modules:
  0.0 508.8 jit_solution(11562974428854957841)
XLA Ops:
  10.0 4.8 all-to-all-start.1
  16.6 7.1 %all-to-all-done.1 = bf16[128,8,256]{0,2,1:T(8,128)(2,1)S(1)} async-done(((bf16[128,8,256]{0,2,1:T(8,128)(2,1)}), bf16[128,8,256]{0,2,1:T(8,128)(2,1)S(1)}, u32[]{:S(2)}, u32[]{:S(2)}) %all-to-all-start.1) | async-done | bytes 524320 | tf_op jit(solution)/shard_map/all_to_all | solution.py:132
  23.7 4.9 all-to-all-start
  30.6 6.9 %all-to-all-done = bf16[128,8,256]{0,2,1:T(8,128)(2,1)S(1)} async-done(((bf16[128,8,256]{0,2,1:T(8,128)(2,1)}), bf16[128,8,256]{0,2,1:T(8,128)(2,1)S(1)}, u32[]{:S(2)}, u32[]{:S(2)}) %all-to-all-start) | async-done | bytes 524320 | tf_op jit(solution)/shard_map/all_to_all | solution.py:131
  38.2 4.8 all-to-all-start.2
  56.5 20.1 %while.10 = (s32[]{:T(128)}, bf16[2,512,2,128]{3,2,1,0:T(2,128)(2,1)}, s32[2]{0:T(128)S(1)}, s32[1024]{0:T(1024)S(1)}, bf16[1024,2,128]{0,2,1:T(8,128)(2,1)}, /*...) while((s32[]{:T(128)}, ...), condition=%wide.region_6.7_spmd, body=%wide.region_3.6_spmd.sunk | while | flops 543949824 | bytes 12077291 | solution.py:63
  58.3 4.7 fusion.76
  63.0 2.4 fusion.77
  68.3 4.7 fusion.76
  73.0 2.4 fusion.77
  78.7 5.1 %all-to-all-start.3 = ((bf16[8,128,256]{2,1,0:T(8,128)(2,1)}), bf16[8,128,256]{2,1,0:T(8,128)(2,1)S(1)}, u32[]{:S(2)}, u32[]{:S(2)}) async-start(bf16[8,128,256]{2,1,0:T(8,128)(2,1)} %all_to_all.67), calls=%async_computation.3 | async-start | bytes 1048576 | tf_op jit(solution)/shard_map/all_to_all | solution.py:167
  83.9 8.9 %convert_reduce_fusion = s32[1536,128]{1,0:T(8,128)} fusion(s32[128,8]{0,1:T(8,128)S(1)} %get-tuple-element.102), kind=kLoop, calls=%fused_computation.32 | loop fusion | flops 4521984 | bytes 790528 | tf_op jit(solution)/shard_map/reduce_sum | solution.py:181
  93.8 5.0 multiply_reduce_fusion
  100.7 5.5 %broadcast_in_dim.51 = bf16[64,2,24,2048]{3,2,1,0:T(8,128)(2,1)} broadcast(bf16[64,24,2048]{2,1,0:T(8,128)(2,1)S(1)} %bitcast.87), dimensions={0,2,3} | broadcast | bytes 18874368 | tf_op jit(solution)/shard_map/broadcast_in_dim | solution.py:189
  106.2 11.6 %all-to-all-start.4 = ((bf16[128,24,2048]{2,1,0:T(8,128)(2,1)}), bf16[128,24,2048]{2,1,0:T(8,128)(2,1)}, u32[]{:S(2)}, u32[]{:S(2)}) async-start(bf16[128,24,2048]{2,1,0:T(8,128)(2,1)} %bitcast.86), calls=%async_computation.4 | async-start | bytes 25165824 | tf_op jit(solution)/shard_map/all_to_all | solution.py:68
  117.8 160.3 %all-to-all-done.4 = bf16[128,24,2048]{2,1,0:T(8,128)(2,1)} async-done(((bf16[128,24,2048]{2,1,0:T(8,128)(2,1)}), bf16[128,24,2048]{2,1,0:T(8,128)(2,1)}, u32[]{:S(2)}, u32[]{:S(2)}) %all-to-all-start.4) | async-done | bytes 12582944 | tf_op jit(solution)/shard_map/all_to_all | solution.py:68
  278.1 17.0 %fusion.38 = f32[3072,1024]{1,0:T(8,128)S(1)} fusion(bf16[3072,2048]{1,0:T(8,128)(2,1)} %bitcast.18, bf16[1,2048,1024]{2,1,0:T(8,128)(2,1)} %param.28), kind=kOutput, calls=%fused_computation.36 | convolution fusion | flops 12884901888 | bytes 29360128 | tf_op jit(solution)/shard_map/dot_general | solution.py:78
  297.3 11.7 %fusion.40 = f32[128,24,2048]{2,0,1:T(8,128)} fusion(bf16[128,24,512]{2,1,0:T(8,128)(2,1)S(1)} %bitcast.98, bf16[1,512,2048]{2,1,0:T(8,128)(2,1)S(1)} %copy-done), kind=kOutput, calls=%fused_computation.38 | convolution fusion | flops 6442450944 | bytes 30408704 | tf_op jit(solution)/shard_map/dot_general | solution.py:83
  309.1 8.4 %dynamic-slice_convert_fusion = bf16[128,12,2048]{2,0,1:T(8,128)(2,1)} fusion(f32[128,24,2048]{2,0,1:T(8,128)} %fusion.40, s32[]{:T(128)S(6)} %select_n.47), kind=kLoop, calls=%fused_computation.28 | loop fusion | bytes 12582916 | tf_op jit(solution)/shard_map/convert_element_type | solution.py:199
  320.0 2.9 reduce
  322.9 4.0 reshape.287
  326.9 13.6 %all-to-all-start.6 = ((bf16[16,2,32768]{2,1,0:T(2,128)(2,1)}), bf16[16,2,32768]{2,1,0:T(2,128)(2,1)S(1)}, u32[]{:S(2)}, u32[]{:S(2)}) async-start(bf16[16,2,32768]{2,1,0:T(2,128)(2,1)} %reshape.287), calls=%async_computation.6 | async-start | bytes 4194304 | tf_op jit(solution)/shard_map/all_to_all | solution.py:149
  340.5 11.8 %add_convert_fusion = bf16[128,12,2048]{2,0,1:T(8,128)(2,1)} fusion(bf16[128,12,2048]{2,0,1:T(8,128)(2,1)} %collective-permute-done, f32[128,24,2048]{2,0,1:T(8,128)} %fusion.40, s32[]{:T(128)S(6)} %select_n.46), kind=kLoop, calls=%fused_computation.27 | loop fusion | flops 9437184 | bytes 25165828 | tf_op jit(solution)/shard_map/convert_element_type | solution.py:200
  352.3 9.7 %copy.108 = bf16[128,12,2048]{2,1,0:T(8,128)(2,1)} copy(bf16[128,12,2048]{2,0,1:T(8,128)(2,1)} %add_convert_fusion) | data formatting | bytes 12582912 | tf_op jit(solution)/shard_map/convert_element_type | solution.py:200
  361.9 12.7 %all-to-all-done.6 = bf16[16,2,32768]{2,1,0:T(2,128)(2,1)S(1)} async-done(((bf16[16,2,32768]{2,1,0:T(2,128)(2,1)}), bf16[16,2,32768]{2,1,0:T(2,128)(2,1)S(1)}, u32[]{:S(2)}, u32[]{:S(2)}) %all-to-all-start.6) | async-done | bytes 2097184 | tf_op jit(solution)/shard_map/all_to_all | solution.py:149
  374.6 5.5 %all-to-all-start.5 = ((bf16[128,12,2048]{2,1,0:T(8,128)(2,1)}), bf16[128,12,2048]{2,1,0:T(8,128)(2,1)}, u32[]{:S(2)}, u32[]{:S(2)}) async-start(bf16[128,12,2048]{2,1,0:T(8,128)(2,1)} %copy.108), calls=%async_computation.5 | async-start | bytes 16777216 | tf_op jit(solution)/shard_map/all_to_all | solution.py:73
  381.0 6.8 %reshape.288 = bf16[16,1,65536]{2,1,0:T(2,128)(2,1)} reshape(bf16[16,2,32768]{2,1,0:T(2,128)(2,1)S(1)} %all-to-all-done.6) | data formatting | bytes 4194304
  387.8 4.5 convolution_convert_fusion.1
  393.5 87.1 %all-to-all-done.5 = bf16[128,12,2048]{2,1,0:T(8,128)(2,1)} async-done(((bf16[128,12,2048]{2,1,0:T(8,128)(2,1)}), bf16[128,12,2048]{2,1,0:T(8,128)(2,1)}, u32[]{:S(2)}, u32[]{:S(2)}) %all-to-all-start.5) | async-done | bytes 6291488 | tf_op jit(solution)/shard_map/all_to_all | solution.py:73
  480.7 10.7 %reshape.267 = bf16[1536,2048]{1,0:T(8,128)(2,1)} reshape(bf16[128,12,2048]{2,1,0:T(8,128)(2,1)} %all-to-all-done.5) | data formatting | bytes 12582912 | tf_op jit(solution)/shard_map/reshape | solution.py:201
  491.4 12.6 %gather_fusion = bf16[1024,2048]{1,0:T(8,128)(2,1)} fusion(bf16[1536,2048]{1,0:T(8,128)(2,1)} %reshape.267, s32[1024]{0:T(1024)S(1)} %broadcast_clamp_fusion), kind=kCustom, calls=%fused_computation | custom fusion | bytes 8392704 | tf_op jit(solution)/shard_map/gather | solution.py:202
  503.9 3.4 fusion.36
  (103 shorter events, 44.8 us)
Async XLA Ops:
  0.6 296.7 %copy-start = (bf16[1,512,2048]{2,1,0:T(8,128)(2,1)S(1)}, bf16[1,512,2048]{2,1,0:T(8,128)(2,1)}, u32[]{:S(2)}) copy-start(bf16[1,512,2048]{2,1,0:T(8,128)(2,1)} %param.29) | copy-start | bytes 6291460
  7.0 36.1 %copy-start.11 = (s32[128,8]{0,1:T(8,128)S(1)}, s32[128,8]{0,1:T(8,128)}, u32[]{:S(2)}) copy-start(s32[128,8]{0,1:T(8,128)} %param.24) | copy-start | bytes 12292
  10.0 13.7 %all-to-all-start.1 = ((bf16[128,8,256]{0,2,1:T(8,128)(2,1)}), bf16[128,8,256]{0,2,1:T(8,128)(2,1)S(1)}, u32[]{:S(2)}, u32[]{:S(2)}) async-start(bf16[128,8,256]{0,2,1:T(8,128)(2,1)} %bitcast.10), calls=%async_computation.1 | async-start | bytes 1048576 | tf_op jit(solution)/shard_map/all_to_all | solution.py:132
  23.7 29.3 %copy-start.3 = (bf16[128,8,256]{0,2,1:T(8,128)(2,1)}, bf16[128,8,256]{0,2,1:T(8,128)(2,1)S(1)}, u32[]{:S(2)}) copy-start(bf16[128,8,256]{0,2,1:T(8,128)(2,1)S(1)} %all-to-all-done.1) | copy-start | bytes 1572868
  23.7 13.8 %all-to-all-start = ((bf16[128,8,256]{0,2,1:T(8,128)(2,1)}), bf16[128,8,256]{0,2,1:T(8,128)(2,1)S(1)}, u32[]{:S(2)}, u32[]{:S(2)}) async-start(bf16[128,8,256]{0,2,1:T(8,128)(2,1)} %bitcast.102), calls=%async_computation | async-start | bytes 1048576 | tf_op jit(solution)/shard_map/all_to_all | solution.py:131
  37.4 0.8 copy-start.7
  38.2 14.8 %all-to-all-start.2 = ((bf16[128,8,256]{0,2,1:T(8,128)(2,1)}), bf16[128,8,256]{0,2,1:T(8,128)(2,1)S(1)}, u32[]{:S(2)}, u32[]{:S(2)}) async-start(bf16[128,8,256]{0,2,1:T(8,128)(2,1)} %bitcast.100), calls=%async_computation.2 | async-start | bytes 1048576 | tf_op jit(solution)/shard_map/all_to_all | solution.py:133
  43.5 13.0 %copy-start.10 = (s32[1024]{0:T(1024)S(1)}, s32[1024]{0:T(1024)}, u32[]{:S(2)}) copy-start(s32[1024]{0:T(1024)} %param.20) | copy-start | bytes 12292
  53.0 3.4 copy-start.5
  63.0 2.4 copy-start.8
  65.7 0.8 copy-start.9
  73.0 2.5 copy-start.8
  75.8 0.8 copy-start.9
  78.7 14.1 %all-to-all-start.3 = ((bf16[8,128,256]{2,1,0:T(8,128)(2,1)}), bf16[8,128,256]{2,1,0:T(8,128)(2,1)S(1)}, u32[]{:S(2)}, u32[]{:S(2)}) async-start(bf16[8,128,256]{2,1,0:T(8,128)(2,1)} %all_to_all.67), calls=%async_computation.3 | async-start | bytes 1048576 | tf_op jit(solution)/shard_map/all_to_all | solution.py:167
  93.8 5.0 copy-start.2
  93.8 5.0 copy-start.13
  106.2 171.9 %all-to-all-start.4 = ((bf16[128,24,2048]{2,1,0:T(8,128)(2,1)}), bf16[128,24,2048]{2,1,0:T(8,128)(2,1)}, u32[]{:S(2)}, u32[]{:S(2)}) async-start(bf16[128,24,2048]{2,1,0:T(8,128)(2,1)} %bitcast.86), calls=%async_computation.4 | async-start | bytes 25165824 | tf_op jit(solution)/shard_map/all_to_all | solution.py:68
  309.1 8.4 %copy-start.12 = (s32[16,8]{0,1:T(8,128)S(1)}, s32[16,8]{0,1:T(8,128)}, u32[]{:S(2)}) copy-start(s32[16,8]{0,1:T(8,128)} %param.23) | copy-start | bytes 1540
  309.1 8.5 %copy-start.4 = (bf16[128,8,256]{0,2,1:T(8,128)(2,1)S(1)}, bf16[128,8,256]{0,2,1:T(8,128)(2,1)}, u32[]{:S(2)}) copy-start(bf16[128,8,256]{0,2,1:T(8,128)(2,1)} %copy-done.3) | copy-start | bytes 1572868
  309.1 8.5 %copy-start.6 = (bf16[128,8,256]{0,2,1:T(8,128)(2,1)S(1)}, bf16[128,8,256]{0,2,1:T(8,128)(2,1)}, u32[]{:S(2)}) copy-start(bf16[128,8,256]{0,2,1:T(8,128)(2,1)} %copy-done.5) | copy-start | bytes 1572868
  317.4 23.1 %collective-permute-start = (bf16[128,12,2048]{2,0,1:T(8,128)(2,1)}, bf16[128,12,2048]{2,0,1:T(8,128)(2,1)}, u32[]{:S(2)}, u32[]{:S(2)}) collective-permute-start(bf16[128,12,2048]{2,0,1:T(8,128)(2,1)} %dynamic-slice_convert_fusion), channel_id=1, source_target_pairs={{0,1},{1,0},{2,3},{3,2},{4,5},{5,4},{6,7},{7,6},{8,9},{9,8},{10,11... | collective-permute-start | bytes 18874376 | tf_op jit(solution)/shard_map/ppermute | solution.py:16
  326.9 47.8 %all-to-all-start.6 = ((bf16[16,2,32768]{2,1,0:T(2,128)(2,1)}), bf16[16,2,32768]{2,1,0:T(2,128)(2,1)S(1)}, u32[]{:S(2)}, u32[]{:S(2)}) async-start(bf16[16,2,32768]{2,1,0:T(2,128)(2,1)} %reshape.287), calls=%async_computation.6 | async-start | bytes 4194304 | tf_op jit(solution)/shard_map/all_to_all | solution.py:149
  361.9 18.4 %copy-start.14 = (f32[128,8]{0,1:T(8,128)S(1)}, f32[128,8]{0,1:T(8,128)}, u32[]{:S(2)}) copy-start(f32[128,8]{0,1:T(8,128)} %param.25) | copy-start | bytes 12292
  361.9 18.5 %copy-start.15 = (s32[16]{0:T(128)S(1)}, s32[16]{0:T(128)}, u32[]{:S(2)}) copy-start(s32[16]{0:T(128)} %param.22) | copy-start | bytes 196
  374.6 106.0 %all-to-all-start.5 = ((bf16[128,12,2048]{2,1,0:T(8,128)(2,1)}), bf16[128,12,2048]{2,1,0:T(8,128)(2,1)}, u32[]{:S(2)}, u32[]{:S(2)}) async-start(bf16[128,12,2048]{2,1,0:T(8,128)(2,1)} %copy.108), calls=%async_computation.5 | async-start | bytes 16777216 | tf_op jit(solution)/shard_map/all_to_all | solution.py:73
  491.4 17.2 %copy-start.1 = (bf16[1,512,2048]{2,1,0:T(8,128)(2,1)S(1)}, bf16[1,512,2048]{2,1,0:T(8,128)(2,1)}, u32[]{:S(2)}) copy-start(bf16[1,512,2048]{2,1,0:T(8,128)(2,1)} %param.29) | copy-start | bytes 6291460
where the time goes:
time: 518 us; the launch traced here: 509 us
  waiting for transfers between devices  274 us (53%)
  local copies, waits for them, and re-layouts  87.7 us (17%)
  matrix products  58.4 us (11%)
  starting transfers between devices  50.3 us (10%)
  other arithmetic  35.5 us (7%)
    all_to_all x1, waiting for transfers between devices, send_rows(): lax.all_to_all(blocks, ('req', 'exp'), split_axis=0, concat_axis=0, tiled...  160 us
    all_to_all x1, waiting for transfers between devices, send_back(): lax.all_to_all(blocks, ('req', 'exp'), split_axis=0, concat_axis=0, tiled...  87.1 us
    dot_general x1, matrix products, half_expert(): projected = jnp.dot(rows, inner_half, preferred_element_type=jnp.float32)  17 us
    unnamed x34, local copies, waits for them, and re-layouts  15.6 us
    all_to_all x1, starting transfers between devices, on_device(): lax.all_to_all(outgoing_pages, 'req', split_axis=0, concat_axis=0, tiled=...  13.6 us
    all_to_all x1, waiting for transfers between devices, on_device(): lax.all_to_all(outgoing_pages, 'req', split_axis=0, concat_axis=0, tiled=...  12.7 us
    gather x1, local copies, waits for them, and re-layouts, on_device(): gathered = returned[slot_index]  12.6 us
    convert_element_type x1, other arithmetic, on_device(): expert_out = (kept + received).astype(jnp.bfloat16)  11.8 us
  transfers between devices with their start and end apart: 8, of which 5 were waited for; matrix products, arithmetic and copies ran while one was open for 13% of the time, Pallas kernels for 0%

commit v1 on v0

--- a/solution.py
+++ b/solution.py
@@ -74,13 +74,25 @@
     return arrived
 
 
-def half_expert(rows, inner_half, outer_half):
+def to_chunks(blocks):
+    count, rows, width = blocks.shape
+    return blocks.reshape(count, 8, rows * width // 8)
+
+
+def from_chunks(blocks, rows, width):
+    return blocks.reshape(blocks.shape[0], rows, width)
+
+
+def gated_units(rows, inner_half):
     projected = jnp.dot(rows, inner_half, preferred_element_type=jnp.float32)
     half_units = projected.shape[1] // 2
-    active = (jax.nn.silu(projected[:, :half_units]) * projected[:, half_units:]).astype(
-        jnp.bfloat16
-    )
-    return jnp.dot(active, outer_half, preferred_element_type=jnp.float32)
+    return (jax.nn.silu(projected[:, :half_units]) * projected[:, half_units:]).astype(jnp.bfloat16)
+
+
+def full_expert(rows, inner_own, outer_own, inner_other, outer_other):
+    own = jnp.dot(gated_units(rows, inner_own), outer_own, preferred_element_type=jnp.float32)
+    other = jnp.dot(gated_units(rows, inner_other), outer_other, preferred_element_type=jnp.float32)
+    return (own + other).astype(jnp.bfloat16)
 
 
 def on_device(
@@ -99,6 +111,8 @@
     expert_inner,
     expert_outer,
 ):
+    partner_inner = partner(expert_inner, "exp", 0)
+    partner_outer = partner(expert_outer, "exp", 0)
     tok_rows, model_width = residual.shape
     req_count = lax.axis_size("req")
     member_count = lax.axis_size("exp")
@@ -111,7 +125,6 @@
     page_count = group_rows // PAGE
     group = lax.axis_index("req")
     member = lax.axis_index("exp")
-    parity = member % 2
     holds_request = (request_groups == group).astype(jnp.int32)
     my_lengths = jnp.sum(holds_request[:, None] * prompt_lengths, axis=0)
     my_pages = jnp.sum(holds_request[:, None] * page_table, axis=0)
@@ -127,11 +140,10 @@
     )
     query_turned = rotate(query_vectors, positions)
     key_turned = rotate(key_vectors, positions)
-    query_group, key_group, value_group = (
-        lax.all_to_all(query_turned, "exp", split_axis=1, concat_axis=0, tiled=True),
-        lax.all_to_all(key_turned, "exp", split_axis=1, concat_axis=0, tiled=True),
-        lax.all_to_all(value_vectors, "exp", split_axis=1, concat_axis=0, tiled=True),
-    )
+    qkv_group = lax.all_to_all(
+        jnp.stack([query_turned, key_turned, value_vectors]), "exp", split_axis=2, concat_axis=1, tiled=True
+    )
+    query_group, key_group, value_group = qkv_group[0], qkv_group[1], qkv_group[2]
     column_count = key_group.shape[1]
     stacked = jnp.stack(
         [
@@ -186,21 +198,24 @@
         .astype(jnp.bfloat16)
         .reshape(expert_count, capacity, model_width)
     )
-    doubled = jnp.broadcast_to(packed[:, None], (expert_count, 2, capacity, model_width)).reshape(
-        device_count, capacity, model_width
-    )
-    expert_input = send_rows(doubled)
-    flat_input = expert_input.reshape(device_count * capacity, model_width)
-    partial_out = half_expert(flat_input, expert_inner[0], expert_outer[0]).reshape(
-        device_count, capacity, model_width
-    )
-    kept = lax.dynamic_slice_in_dim(partial_out, parity * half_capacity, half_capacity, 1)
-    handed = lax.dynamic_slice_in_dim(partial_out, (1 - parity) * half_capacity, half_capacity, 1)
-    received = partner(handed.astype(jnp.bfloat16), "exp", 0).astype(handed.dtype)
-    expert_out = (kept + received).astype(jnp.bfloat16)
-    returned = send_back(expert_out).reshape(expert_count * capacity, model_width)
-    gathered = returned[slot_index]
-    mixed = jnp.einsum("tk,tkd->td", gate_weights, gathered.astype(jnp.float32))
+    outgoing = to_chunks(packed.reshape(device_count, half_capacity, model_width))
+    expert_input = from_chunks(send_rows(outgoing), half_capacity, model_width)
+    flat_input = expert_input.reshape(device_count * half_capacity, model_width)
+    expert_out = full_expert(
+        flat_input, expert_inner[0], expert_outer[0], partner_inner[0], partner_outer[0]
+    ).reshape(device_count, half_capacity, model_width)
+    returned = from_chunks(send_back(to_chunks(expert_out)), half_capacity, model_width).reshape(
+        expert_count * capacity, model_width
+    )
+    combine = jnp.sum(
+        jnp.where(slot_index[:, :, None] == slot_range[None, None, :], gate_weights[:, :, None], 0.0),
+        axis=1,
+    )
+    combine_high = combine.astype(jnp.bfloat16)
+    combine_low = (combine - combine_high.astype(jnp.float32)).astype(jnp.bfloat16)
+    mixed = jnp.dot(combine_high, returned, preferred_element_type=jnp.float32) + jnp.dot(
+        combine_low, returned, preferred_element_type=jnp.float32
+    )
     layer_out = (hidden + mixed).astype(jnp.bfloat16)
     return (layer_out, kv_pages)
 

time: 518 us -> 368 us (0.71)
  waiting for transfers between devices: 274 us -> 152 us
  other arithmetic: 35.5 us -> 18 us
  starting transfers between devices: 50.3 us -> 34.4 us
  matrix products: 58.4 us -> 70.2 us
    all_to_all x1, waiting for transfers between devices: 160 us -> 66.5 us  [send_rows(): lax.all_to_all(blocks, ('req', 'exp'), split_axis=0, concat_axis=0, tiled...]
    another operation x0 -> x9, local copies, waits for them, and re-layouts: none -> 54.4 us  [the longest x2 21.1 us: to_chunks(): return blocks.reshape(count, 8, rows * width // 8)]
    all_to_all x1, waiting for transfers between devices: 87.1 us -> 59.9 us  [send_back(): lax.all_to_all(blocks, ('req', 'exp'), split_axis=0, concat_axis=0, tiled...]
    convert_element_type x2 -> x0, local copies, waits for them, and re-layouts: 18 us -> none  [the longest x1 9.65 us: on_device(): expert_out = (kept + received).astype(jnp.bfloat16)]
    reshape x4 -> x0, local copies, waits for them, and re-layouts: 16.1 us -> none  [the longest x1 10.7 us: on_device(): send_back(expert_out).reshape(expert_count * capacity, model_width)]
    convert_element_type x3 -> x0, other arithmetic: 15.2 us -> none  [the longest x1 11.8 us: on_device(): expert_out = (kept + received).astype(jnp.bfloat16)]
    all_to_all x1, waiting for transfers between devices: 12.7 us -> 0.01 us  [on_device(): lax.all_to_all(outgoing_pages, 'req', split_axis=0, concat_axis=0, tiled=...]
    gather x1 -> x0, local copies, waits for them, and re-layouts: 12.6 us -> none  [on_device(): gathered = returned[slot_index]]
  transfers between devices with their start and end apart: 8 -> 7, of which waited for: 5 -> 4; matrix products, arithmetic and copies ran while one was open for 13% -> 25% of each run, Pallas kernels for 0% -> 0%
where the time goes in v1:
time: 368 us; the launch traced here: 361 us
  waiting for transfers between devices  152 us (41%)
  local copies, waits for them, and re-layouts  83.3 us (23%)
  matrix products  70.2 us (19%)
  starting transfers between devices  34.4 us (9%)
  other arithmetic  18 us (5%)
    all_to_all x1, waiting for transfers between devices, send_rows(): lax.all_to_all(blocks, ('req', 'exp'), split_axis=0, concat_axis=0, tiled...  66.5 us
    all_to_all x1, waiting for transfers between devices, send_back(): lax.all_to_all(blocks, ('req', 'exp'), split_axis=0, concat_axis=0, tiled...  59.9 us
    all_to_all x1, waiting for transfers between devices, on_device(): lax.all_to_all(jnp.stack([query_turned, key_turned, value_vectors]), 'exp...  25.3 us
    another operation x2, local copies, waits for them, and re-layouts, to_chunks(): return blocks.reshape(count, 8, rows * width // 8)  21.1 us
    dot_general x2, matrix products, gated_units(): projected = jnp.dot(rows, inner_half, preferred_element_type=jnp.float32)  20.8 us
    unnamed x25, local copies, waits for them, and re-layouts  13.3 us
    another operation x2, local copies, waits for them, and re-layouts, on_device(): jnp.stack([query_turned, key_turned, value_vectors])  12.1 us
    another operation x1, local copies, waits for them, and re-layouts, on_device(): flat_input = expert_input.reshape(device_count * half_capacity, model_width)  10.5 us
  transfers between devices with their start and end apart: 7, of which 4 were waited for; matrix products, arithmetic and copies ran while one was open for 25% of the time, Pallas kernels for 0%

profile of v1, /device:TPU:2, one launch (start us, length us, event | category | flops | bytes accessed | tf_op | source)
XLA Modules:
  0.0 361.3 jit_solution(2779627470354529943)
XLA Ops:
  7.8 10.8 %copy.96 = bf16[3,128,2048]{1,0,2:T(4,128)(2,1)} copy(bf16[3,128,2048]{1,2,0:T(8,128)(2,1)S(1)} %pad_maximum_fusion) | data formatting | bytes 3145728 | tf_op jit(solution)/shard_map/stack | solution.py:144
  18.5 5.4 %all-to-all-start = ((bf16[3,128,2048]{1,0,2:T(4,128)(2,1)}), bf16[3,128,2048]{1,0,2:T(4,128)(2,1)S(1)}, u32[]{:S(2)}, u32[]{:S(2)}) async-start(bf16[3,128,2048]{1,0,2:T(4,128)(2,1)} %copy.96), calls=%async_computation | async-start | bytes 4194304 | tf_op jit(solution)/shard_map/all_to_all | solution.py:143
  24.3 25.3 %all-to-all-done = bf16[3,128,2048]{1,0,2:T(4,128)(2,1)S(1)} async-done(((bf16[3,128,2048]{1,0,2:T(4,128)(2,1)}), bf16[3,128,2048]{1,0,2:T(4,128)(2,1)S(1)}, u32[]{:S(2)}, u32[]{:S(2)}) %all-to-all-start) | async-done | bytes 1572896 | tf_op jit(solution)/shard_map/all_to_all | solution.py:143
  49.6 2.4 copy.97
  55.0 20.0 %while.10 = (s32[]{:T(128)}, bf16[2,512,2,128]{3,2,1,0:T(2,128)(2,1)}, s32[2]{0:T(128)S(1)}, s32[1024]{0:T(1024)S(1)}, bf16[1024,2,128]{2,1,0:T(2,128)(2,1)S(1)}...) while((s32[]{:T(128)}, ...), condition=%wide.region_6.7_spmd, body=%wide.region_3.6_spmd.sunk | while | flops 543949824 | bytes 12077299 | solution.py:63
  57.0 4.5 %fusion.85 = (f32[2,512]{1,0:T(2,128)S(1)}, bf16[2,512,1024]{2,1,0:T(8,128)(2,1)}) fusion(pred[512,1024]{1,0:T(8,128)(4,1)S(1)} %broadcast_compare_fusion.2, bf16[1024,2,128]{2,0,1:T(8,128)(2,1)} %get-tuple-element.196, bf16[512,2,128]{2,1,0:T(2,128)(2,1)S(1)} %constant_dynamic-slice_fusion.2), kind=kOutput, calls=%fused_computation.98.clone.1 | convolution fusion | flops 274727936 | bytes 3411968 | tf_op jit(solution)/shard_map/while/body/eval_jaxpr/sub | solution.py:53
  61.6 2.4 fusion.86
  67.0 4.5 %fusion.85 = (f32[2,512]{1,0:T(2,128)S(1)}, bf16[2,512,1024]{2,1,0:T(8,128)(2,1)}) fusion(pred[512,1024]{1,0:T(8,128)(4,1)S(1)} %broadcast_compare_fusion.2, bf16[1024,2,128]{2,0,1:T(8,128)(2,1)} %get-tuple-element.196, bf16[512,2,128]{2,1,0:T(2,128)(2,1)S(1)} %constant_dynamic-slice_fusion.2), kind=kOutput, calls=%fused_computation.98.clone.1 | convolution fusion | flops 274727936 | bytes 3411968 | tf_op jit(solution)/shard_map/while/body/eval_jaxpr/sub | solution.py:53
  71.5 2.4 fusion.86
  77.2 5.1 %all-to-all-start.1 = ((bf16[8,128,256]{2,1,0:T(8,128)(2,1)}), bf16[8,128,256]{2,1,0:T(8,128)(2,1)S(1)}, u32[]{:S(2)}, u32[]{:S(2)}) async-start(bf16[8,128,256]{2,1,0:T(8,128)(2,1)} %all_to_all.42), calls=%async_computation.1 | async-start | bytes 1048576 | tf_op jit(solution)/shard_map/all_to_all | solution.py:179
  82.3 8.0 %convert_reduce_fusion = s32[1536,128]{1,0:T(8,128)S(1)} fusion(s32[128,8]{0,1:T(8,128)S(1)} %multiply_add_fusion), kind=kLoop, calls=%fused_computation.27 | loop fusion | flops 4521984 | bytes 790528 | tf_op jit(solution)/shard_map/reduce_sum | solution.py:193
  91.4 4.8 %multiply_reduce_fusion = (f32[128]{0:T(128)S(1)}, f32[128,2048]{1,0:T(8,128)S(1)}) fusion(bf16[128,2048]{0,1:T(8,128)(2,1)S(1)} %bitcast.89, bf16[2048,2048]{1,0:T(8,128)(2,1)} %param.26, bf16[128,2048]{1,0:T(8,128)(2,1)} %param.16), kind=kOutput, calls=%fused_computation.53 | convolution fusion | flops 1074790272 | bytes 10486272 | tf_op jit(solution)/shard_map/dot_general | solution.py:180
  96.2 4.5 %convolution_convert_fusion.2 = bf16[1536,2048]{1,0:T(8,128)(2,1)} fusion(f32[128,2048]{1,0:T(8,128)S(1)} %get-tuple-element.117, f32[2048]{0:T(1024)S(1)} %copy-done.8, f32[128]{0:T(128)S(1)} %add_rsqrt_fusion, s32[1536,128]{1,0:T(8,128)S(1)} %convert_reduce_fusion), kind=kOutput, calls=%fused_computation.26 | convolution fusion | flops 809435136 | bytes 8135168 | tf_op jit(solution)/shard_map/dot_general | solution.py:197
  100.7 10.5 %reshape_reshape_reshape.3 = bf16[128,8,3072]{2,1,0:T(8,128)(2,1)} reshape(bf16[1536,2048]{1,0:T(8,128)(2,1)} %convolution_convert_fusion.2) | data formatting | bytes 12582912 | tf_op jit(solution)/shard_map/reshape;reshape;reshape | solution.py:79
  111.3 10.1 %all-to-all-start.2 = ((bf16[128,8,3072]{2,1,0:T(8,128)(2,1)}), bf16[128,8,3072]{2,1,0:T(8,128)(2,1)}, u32[]{:S(2)}, u32[]{:S(2)}) async-start(bf16[128,8,3072]{2,1,0:T(8,128)(2,1)} %reshape_reshape_reshape.3), calls=%async_computation.2 | async-start | bytes 12582912 | tf_op jit(solution)/shard_map/all_to_all | solution.py:68
  124.0 2.9 reduce
  127.0 4.0 %reshape.264 = bf16[16,2,32768]{2,1,0:T(2,128)(2,1)} reshape(bf16[16,65536]{1,0:T(8,128)(2,1)} %reduce) | data formatting | bytes 4194304
  131.0 66.5 %all-to-all-done.2 = bf16[128,8,3072]{2,1,0:T(8,128)(2,1)} async-done(((bf16[128,8,3072]{2,1,0:T(8,128)(2,1)}), bf16[128,8,3072]{2,1,0:T(8,128)(2,1)}, u32[]{:S(2)}, u32[]{:S(2)}) %all-to-all-start.2) | async-done | bytes 6291488 | tf_op jit(solution)/shard_map/all_to_all | solution.py:68
  197.5 4.1 %all-to-all-start.4 = ((bf16[16,2,32768]{2,1,0:T(2,128)(2,1)}), bf16[16,2,32768]{2,1,0:T(2,128)(2,1)S(1)}, u32[]{:S(2)}, u32[]{:S(2)}) async-start(bf16[16,2,32768]{2,1,0:T(2,128)(2,1)} %reshape.264), calls=%async_computation.4 | async-start | bytes 4194304 | tf_op jit(solution)/shard_map/all_to_all | solution.py:161
  201.7 10.5 %reshape_reshape.9 = bf16[1536,2048]{1,0:T(8,128)(2,1)} reshape(bf16[128,8,3072]{2,1,0:T(8,128)(2,1)} %all-to-all-done.2) | data formatting | bytes 12582912 | tf_op jit(solution)/shard_map/reshape;reshape | solution.py:203
  212.1 10.1 %fusion.33 = f32[1536,1024]{1,0:T(8,128)S(1)} fusion(bf16[1536,2048]{1,0:T(8,128)(2,1)} %reshape_reshape.9, bf16[1,2048,1024]{2,1,0:T(8,128)(2,1)} %param.28), kind=kOutput, calls=%fused_computation.33 | convolution fusion | flops 6442450944 | bytes 16777216 | tf_op jit(solution)/shard_map/dot_general | solution.py:87
  222.3 10.7 %fusion.31 = f32[1536,1024]{1,0:T(8,128)S(1)} fusion(bf16[1536,2048]{1,0:T(8,128)(2,1)S(1)} %copy-done.2, bf16[1,2048,1024]{2,1,0:T(8,128)(2,1)} %collective-permute-done), kind=kOutput, calls=%fused_computation.31 | convolution fusion | flops 6442450944 | bytes 16777216 | tf_op jit(solution)/shard_map/dot_general | solution.py:87
  233.0 6.4 %fusion.42 = f32[1536,2048]{1,0:T(8,128)} fusion(bf16[1,512,2048]{2,1,0:T(8,128)(2,1)S(1)} %copy-done.11, f32[1536,1024]{1,0:T(8,128)S(1)} %fusion.33), kind=kOutput, calls=%fused_computation.46 | convolution fusion | flops 3225944064 | bytes 20971520 | tf_op jit(solution)/shard_map/dot_general | solution.py:93
  239.4 8.8 %add_convert_fusion = bf16[1536,2048]{1,0:T(8,128)(2,1)} fusion(f32[1536,2048]{1,0:T(8,128)} %fusion.42, bf16[1,512,2048]{2,1,0:T(8,128)(2,1)} %collective-permute-done.1, f32[1536,1024]{1,0:T(8,128)S(1)} %fusion.31), kind=kOutput, calls=%fused_computation.25 | convolution fusion | flops 3232235520 | bytes 27262976 | tf_op jit(solution)/shard_map/dot_general | solution.py:94
  248.2 10.5 %reshape_reshape.10 = bf16[128,8,3072]{2,1,0:T(8,128)(2,1)} reshape(bf16[1536,2048]{1,0:T(8,128)(2,1)} %add_convert_fusion) | data formatting | bytes 12582912 | tf_op jit(solution)/shard_map/reshape;reshape | solution.py:79
  258.7 9.1 %all-to-all-start.3 = ((bf16[128,8,3072]{2,1,0:T(8,128)(2,1)}), bf16[128,8,3072]{2,1,0:T(8,128)(2,1)}, u32[]{:S(2)}, u32[]{:S(2)}) async-start(bf16[128,8,3072]{2,1,0:T(8,128)(2,1)} %reshape_reshape.10), calls=%async_computation.3 | async-start | bytes 12582912 | tf_op jit(solution)/shard_map/all_to_all | solution.py:73
  268.6 2.9 select_reduce_fusion
  271.5 6.7 %reshape.265 = bf16[16,1,65536]{2,1,0:T(2,128)(2,1)} reshape(bf16[16,2,32768]{2,1,0:T(2,128)(2,1)S(1)} %all-to-all-done.4) | data formatting | bytes 4194304
  278.3 4.5 %convolution_convert_fusion.1 = bf16[8,65536]{1,0:T(8,128)(2,1)S(1)} fusion(bf16[16,1,65536]{2,1,0:T(2,128)(2,1)} %reshape.265, s32[8,16]{1,0:T(8,128)S(1)} %convert_reduce_fusion.2), kind=kOutput, calls=%fused_computation.24 | convolution fusion | flops 17301632 | bytes 3146240 | tf_op jit(solution)/shard_map/dot_general | solution.py:169
  284.0 59.9 %all-to-all-done.3 = bf16[128,8,3072]{2,1,0:T(8,128)(2,1)} async-done(((bf16[128,8,3072]{2,1,0:T(8,128)(2,1)}), bf16[128,8,3072]{2,1,0:T(8,128)(2,1)}, u32[]{:S(2)}, u32[]{:S(2)}) %all-to-all-start.3) | async-done | bytes 6291488 | tf_op jit(solution)/shard_map/all_to_all | solution.py:73
  343.9 10.4 %reshape_reshape.11 = bf16[1536,2048]{1,0:T(8,128)(2,1)} reshape(bf16[128,8,3072]{2,1,0:T(8,128)(2,1)} %all-to-all-done.3) | data formatting | bytes 12582912 | tf_op jit(solution)/shard_map/reshape;reshape | solution.py:207
  354.3 3.9 %fusion.52 = f32[128,2048]{1,0:T(8,128)S(1)} fusion(bf16[1536,2048]{1,0:T(8,128)(2,1)} %reshape_reshape.11, f32[128,1536]{1,0:T(8,128)S(1)} %copy-done.1), kind=kOutput, calls=%fused_computation.68 | convolution fusion | flops 805502976 | bytes 8126464 | tf_op jit(solution)/shard_map/dot_general | solution.py:216
  (92 shorter events, 25.6 us)
Async XLA Ops:
  7.8 16.2 %copy-start.6 = (s32[128,8]{0,1:T(8,128)S(1)}, s32[128,8]{0,1:T(8,128)}, u32[]{:S(2)}) copy-start(s32[128,8]{0,1:T(8,128)} %param.24) | copy-start | bytes 12292
  18.5 31.1 %all-to-all-start = ((bf16[3,128,2048]{1,0,2:T(4,128)(2,1)}), bf16[3,128,2048]{1,0,2:T(4,128)(2,1)S(1)}, u32[]{:S(2)}, u32[]{:S(2)}) async-start(bf16[3,128,2048]{1,0,2:T(4,128)(2,1)} %copy.96), calls=%async_computation | async-start | bytes 4194304 | tf_op jit(solution)/shard_map/all_to_all | solution.py:143
  52.0 3.0 copy-start.5
  61.6 2.4 copy-start.3
  64.2 0.8 copy-start.4
  71.5 2.4 copy-start.3
  74.2 0.8 copy-start.4
  77.2 13.9 %all-to-all-start.1 = ((bf16[8,128,256]{2,1,0:T(8,128)(2,1)}), bf16[8,128,256]{2,1,0:T(8,128)(2,1)S(1)}, u32[]{:S(2)}, u32[]{:S(2)}) async-start(bf16[8,128,256]{2,1,0:T(8,128)(2,1)} %all_to_all.42), calls=%async_computation.1 | async-start | bytes 1048576 | tf_op jit(solution)/shard_map/all_to_all | solution.py:179
  91.4 4.8 %copy-start.8 = (f32[2048]{0:T(1024)S(1)}, f32[2048]{0:T(1024)}, u32[]{:S(2)}) copy-start(f32[2048]{0:T(1024)} %param.27) | copy-start | bytes 24580
  111.3 10.7 %copy-start.7 = (s32[16,8]{0,1:T(8,128)S(1)}, s32[16,8]{0,1:T(8,128)}, u32[]{:S(2)}) copy-start(s32[16,8]{0,1:T(8,128)} %param.23) | copy-start | bytes 1540
  111.3 86.2 %all-to-all-start.2 = ((bf16[128,8,3072]{2,1,0:T(8,128)(2,1)}), bf16[128,8,3072]{2,1,0:T(8,128)(2,1)}, u32[]{:S(2)}, u32[]{:S(2)}) async-start(bf16[128,8,3072]{2,1,0:T(8,128)(2,1)} %reshape_reshape_reshape.3), calls=%async_computation.2 | async-start | bytes 12582912 | tf_op jit(solution)/shard_map/all_to_all | solution.py:68
  121.4 100.8 %collective-permute-start = (bf16[1,2048,1024]{2,1,0:T(8,128)(2,1)}, bf16[1,2048,1024]{2,1,0:T(8,128)(2,1)}, u32[]{:S(2)}, u32[]{:S(2)}) collective-permute-start(bf16[1,2048,1024]{2,1,0:T(8,128)(2,1)} %param.28), channel_id=1, source_target_pairs={{0,1},{1,0},{2,3},{3,2},{4,5},{5,4},{6,7},{7,6},{8,9},{9,8},{10,11... | collective-permute-start | bytes 12582920 | tf_op jit(solution)/shard_map/ppermute | solution.py:16
  121.6 117.8 %collective-permute-start.1 = (bf16[1,512,2048]{2,1,0:T(8,128)(2,1)}, bf16[1,512,2048]{2,1,0:T(8,128)(2,1)}, u32[]{:S(2)}, u32[]{:S(2)}) collective-permute-start(bf16[1,512,2048]{2,1,0:T(8,128)(2,1)} %param.29), channel_id=1, source_target_pairs={{0,1},{1,0},{2,3},{3,2},{4,5},{5,4},{6,7},{7,6},{8,9},{9,8},{10,11... | collective-permute-start | bytes 6291464 | tf_op jit(solution)/shard_map/ppermute | solution.py:16
  197.5 61.2 %all-to-all-start.4 = ((bf16[16,2,32768]{2,1,0:T(2,128)(2,1)}), bf16[16,2,32768]{2,1,0:T(2,128)(2,1)S(1)}, u32[]{:S(2)}, u32[]{:S(2)}) async-start(bf16[16,2,32768]{2,1,0:T(2,128)(2,1)} %reshape.264), calls=%async_computation.4 | async-start | bytes 4194304 | tf_op jit(solution)/shard_map/all_to_all | solution.py:161
  212.1 10.2 %copy-start.2 = (bf16[1536,2048]{1,0:T(8,128)(2,1)S(1)}, bf16[1536,2048]{1,0:T(8,128)(2,1)}, u32[]{:S(2)}) copy-start(bf16[1536,2048]{1,0:T(8,128)(2,1)} %reshape_reshape.9) | copy-start | bytes 18874372
  222.2 10.7 %copy-start.11 = (bf16[1,512,2048]{2,1,0:T(8,128)(2,1)S(1)}, bf16[1,512,2048]{2,1,0:T(8,128)(2,1)}, u32[]{:S(2)}) copy-start(bf16[1,512,2048]{2,1,0:T(8,128)(2,1)} %param.29) | copy-start | bytes 6291460
  258.7 9.2 %copy-start.10 = (s32[16]{0:T(128)S(1)}, s32[16]{0:T(128)}, u32[]{:S(2)}) copy-start(s32[16]{0:T(128)} %param.22) | copy-start | bytes 196
  258.7 9.6 %copy-start.9 = (f32[128,8]{0,1:T(8,128)S(1)}, f32[128,8]{0,1:T(8,128)}, u32[]{:S(2)}) copy-start(f32[128,8]{0,1:T(8,128)} %param.25) | copy-start | bytes 12292
  258.7 85.1 %all-to-all-start.3 = ((bf16[128,8,3072]{2,1,0:T(8,128)(2,1)}), bf16[128,8,3072]{2,1,0:T(8,128)(2,1)}, u32[]{:S(2)}, u32[]{:S(2)}) async-start(bf16[128,8,3072]{2,1,0:T(8,128)(2,1)} %reshape_reshape.10), calls=%async_computation.3 | async-start | bytes 12582912 | tf_op jit(solution)/shard_map/all_to_all | solution.py:73
  284.0 70.3 %copy-start.1 = (f32[128,1536]{1,0:T(8,128)S(1)}, f32[128,1536]{1,0:T(8,128)}, u32[]{:S(2)}) copy-start(f32[128,1536]{1,0:T(8,128)} %select_reduce_fusion) | copy-start | bytes 2359300
  354.3 4.6 %copy-start = (bf16[1536,2048]{1,0:T(8,128)(2,1)S(1)}, bf16[1536,2048]{1,0:T(8,128)(2,1)}, u32[]{:S(2)}) copy-start(bf16[1536,2048]{1,0:T(8,128)(2,1)} %reshape_reshape.11) | copy-start | bytes 18874372

commit v2 on v1

--- a/solution.py
+++ b/solution.py
@@ -1,10 +1,13 @@
 import jax
 import jax.numpy as jnp
 from jax import lax
-from jax.sharding import PartitionSpec as P
+from jax.sharding import Mesh, PartitionSpec as P
 
 HEAD = 128
 PAGE = 128
+MEMBER = ("x", "core")
+EXPERT_AXES = ("req", "x")
+EVERY = ("req", "x", "core")
 
 
 rope_base = 10000.0
@@ -65,22 +68,13 @@
 
 
 def send_rows(blocks):
-    arrived = lax.all_to_all(blocks, ("req", "exp"), split_axis=0, concat_axis=0, tiled=True)
+    arrived = lax.all_to_all(blocks, EXPERT_AXES, split_axis=0, concat_axis=0, tiled=True)
     return arrived
 
 
 def send_back(blocks):
-    arrived = lax.all_to_all(blocks, ("req", "exp"), split_axis=0, concat_axis=0, tiled=True)
+    arrived = lax.all_to_all(blocks, EXPERT_AXES, split_axis=0, concat_axis=0, tiled=True)
     return arrived
-
-
-def to_chunks(blocks):
-    count, rows, width = blocks.shape
-    return blocks.reshape(count, 8, rows * width // 8)
-
-
-def from_chunks(blocks, rows, width):
-    return blocks.reshape(blocks.shape[0], rows, width)
 
 
 def gated_units(rows, inner_half):
@@ -111,20 +105,19 @@
     expert_inner,
     expert_outer,
 ):
-    partner_inner = partner(expert_inner, "exp", 0)
-    partner_outer = partner(expert_outer, "exp", 0)
+    partner_inner = partner(expert_inner, "core", 0)
+    partner_outer = partner(expert_outer, "core", 0)
     tok_rows, model_width = residual.shape
     req_count = lax.axis_size("req")
-    member_count = lax.axis_size("exp")
+    member_count = lax.axis_size("x") * lax.axis_size("core")
     device_count = req_count * member_count
     expert_count = device_count // 2
     group_rows = tok_rows * member_count
     top_count = expert_ids.shape[1]
     capacity = 3 * tok_rows * top_count // (2 * expert_count)
-    half_capacity = capacity // 2
     page_count = group_rows // PAGE
     group = lax.axis_index("req")
-    member = lax.axis_index("exp")
+    member = lax.axis_index(MEMBER)
     holds_request = (request_groups == group).astype(jnp.int32)
     my_lengths = jnp.sum(holds_request[:, None] * prompt_lengths, axis=0)
     my_pages = jnp.sum(holds_request[:, None] * page_table, axis=0)
@@ -140,10 +133,13 @@
     )
     query_turned = rotate(query_vectors, positions)
     key_turned = rotate(key_vectors, positions)
+    head_chunks = jnp.stack([query_turned, key_turned, value_vectors]).reshape(
+        3, tok_rows, member_count, model_width // member_count
+    )
     qkv_group = lax.all_to_all(
-        jnp.stack([query_turned, key_turned, value_vectors]), "exp", split_axis=2, concat_axis=1, tiled=True
-    )
-    query_group, key_group, value_group = qkv_group[0], qkv_group[1], qkv_group[2]
+        head_chunks.transpose(0, 2, 1, 3), MEMBER, split_axis=1, concat_axis=2, tiled=True
+    )
+    query_group, key_group, value_group = qkv_group[0, 0], qkv_group[1, 0], qkv_group[2, 0]
     column_count = key_group.shape[1]
     stacked = jnp.stack(
         [
@@ -176,7 +172,7 @@
     value_heads = value_group.reshape(group_rows, heads_here, HEAD)
     block_rows = min(512, group_rows)
     attended = attend_all(query_heads, key_heads, value_heads, segment_ids, block_rows)
-    token_heads = lax.all_to_all(attended, "exp", split_axis=0, concat_axis=1, tiled=True)
+    token_heads = lax.all_to_all(attended, MEMBER, split_axis=0, concat_axis=1, tiled=True)
     hidden = residual.astype(jnp.float32) + jnp.dot(
         token_heads, out_weight, preferred_element_type=jnp.float32
     )
@@ -198,15 +194,12 @@
         .astype(jnp.bfloat16)
         .reshape(expert_count, capacity, model_width)
     )
-    outgoing = to_chunks(packed.reshape(device_count, half_capacity, model_width))
-    expert_input = from_chunks(send_rows(outgoing), half_capacity, model_width)
-    flat_input = expert_input.reshape(device_count * half_capacity, model_width)
+    expert_input = send_rows(packed)
+    flat_input = expert_input.reshape(expert_count * capacity, model_width)
     expert_out = full_expert(
         flat_input, expert_inner[0], expert_outer[0], partner_inner[0], partner_outer[0]
-    ).reshape(device_count, half_capacity, model_width)
-    returned = from_chunks(send_back(to_chunks(expert_out)), half_capacity, model_width).reshape(
-        expert_count * capacity, model_width
-    )
+    ).reshape(expert_count, capacity, model_width)
+    returned = send_back(expert_out).reshape(expert_count * capacity, model_width)
     combine = jnp.sum(
         jnp.where(slot_index[:, :, None] == slot_range[None, None, :], gate_weights[:, :, None], 0.0),
         axis=1,
@@ -221,26 +214,29 @@
 
 
 def solution(mesh):
+    req_count, member_count = mesh.devices.shape
+    fine = Mesh(mesh.devices.reshape(req_count, member_count // 2, 2), EVERY)
+    token_rows = P(EVERY, None)
     placed = (
-        P(("req", "exp"), None),
-        P(("req", "exp"), None),
-        P(("req", "exp"), None),
-        P(("req", "exp"), None),
+        token_rows,
+        token_rows,
+        token_rows,
+        token_rows,
         P("req"),
         P(),
         P(),
         P(),
-        P(("req", "exp"), None),
-        P(("req", "exp"), None),
-        P(),
-        P(),
-        P(("req", "exp"), None, None),
-        P(("req", "exp"), None, None),
+        token_rows,
+        token_rows,
+        P(),
+        P(),
+        P(EVERY, None, None),
+        P(EVERY, None, None),
     )
     return jax.shard_map(
         on_device,
-        mesh=mesh,
+        mesh=fine,
         in_specs=placed,
-        out_specs=(P(("req", "exp"), None), P("req", None, None, "exp")),
+        out_specs=(token_rows, P("req", None, None, MEMBER)),
         check_vma=False,
     )

time: 368 us -> 325 us (0.88)
  local copies, waits for them, and re-layouts: 83.3 us -> 29.6 us
  starting transfers between devices: 34.4 us -> 42.1 us
  waiting for transfers between devices: 152 us -> 157 us
    another operation x6 -> x0, local copies, waits for them, and re-layouts: 54 us -> none  [the longest x2 21.1 us: to_chunks(): return blocks.reshape(count, 8, rows * width // 8)]
    all_to_all x1, starting transfers between devices: 4.14 us -> 9.72 us  [on_device(): lax.all_to_all(outgoing_pages, 'req', split_axis=0, concat_axis=0, tiled=...]
    all_to_all x4, waiting for transfers between devices: 152 us -> 157 us  [the longest x1 71.9 us: send_rows(): lax.all_to_all(blocks, EXPERT_AXES, split_axis=0, concat_axis=0, tiled=True)]
    unnamed x25 -> x24, local copies, waits for them, and re-layouts: 13.3 us -> 14 us
  transfers between devices with their start and end apart: 7 -> 7, of which waited for: 4 -> 4; matrix products, arithmetic and copies ran while one was open for 25% -> 22% of each run, Pallas kernels for 0% -> 0%
where the time goes in v2:
time: 325 us; the launch traced here: 319 us
  waiting for transfers between devices  157 us (48%)
  matrix products  70.2 us (22%)
  starting transfers between devices  42.1 us (13%)
  local copies, waits for them, and re-layouts  29.6 us (9%)
  other arithmetic  18 us (6%)
    all_to_all x1, waiting for transfers between devices, send_rows(): lax.all_to_all(blocks, EXPERT_AXES, split_axis=0, concat_axis=0, tiled=True)  71.9 us
    all_to_all x1, waiting for transfers between devices, send_back(): lax.all_to_all(blocks, EXPERT_AXES, split_axis=0, concat_axis=0, tiled=True)  64.6 us
    dot_general x2, matrix products, gated_units(): projected = jnp.dot(rows, inner_half, preferred_element_type=jnp.float32)  20.1 us
    all_to_all x1, waiting for transfers between devices, on_device(): lax.all_to_all(head_chunks.transpose(0, 2, 1, 3), MEMBER, split_axis=1, c...  19.7 us
    unnamed x24, local copies, waits for them, and re-layouts  14 us
    all_to_all x1, starting transfers between devices, send_back(): lax.all_to_all(blocks, EXPERT_AXES, split_axis=0, concat_axis=0, tiled=True)  11.1 us
    all_to_all x1, starting transfers between devices, send_rows(): lax.all_to_all(blocks, EXPERT_AXES, split_axis=0, concat_axis=0, tiled=True)  11 us
    all_to_all x1, starting transfers between devices, on_device(): lax.all_to_all(outgoing_pages, 'req', split_axis=0, concat_axis=0, tiled=...  9.72 us
  transfers between devices with their start and end apart: 7, of which 4 were waited for; matrix products, arithmetic and copies ran while one was open for 22% of the time, Pallas kernels for 0%

profile of v2, /device:TPU:2, one launch (start us, length us, event | category | flops | bytes accessed | tf_op | source)
XLA Modules:
  0.0 319.4 jit_solution(15194584150198190323)
XLA Ops:
  3.2 1.3 copy.96
  4.5 1.2 copy.94
  7.8 1.3 copy.97
  9.0 4.8 %all-to-all-start = ((bf16[3,8,128,256]{2,3,0,1:T(8,128)(2,1)}), bf16[3,8,128,256]{2,3,0,1:T(8,128)(2,1)S(1)}, u32[]{:S(2)}, u32[]{:S(2)}) async-start(bf16[3,8,128,256]{2,3,0,1:T(8,128)(2,1)} %copy.97), calls=%async_computation | async-start | bytes 3145728 | tf_op jit(solution)/shard_map/all_to_all | solution.py:139
  14.2 19.7 %all-to-all-done = bf16[3,8,128,256]{2,3,0,1:T(8,128)(2,1)S(1)} async-done(((bf16[3,8,128,256]{2,3,0,1:T(8,128)(2,1)}), bf16[3,8,128,256]{2,3,0,1:T(8,128)(2,1)S(1)}, u32[]{:S(2)}, u32[]{:S(2)}) %all-to-all-start) | async-done | bytes 1572896 | tf_op jit(solution)/shard_map/all_to_all | solution.py:139
  34.0 1.3 slice_bitcast_fusion
  37.6 17.7 %while.10 = (s32[]{:T(128)}, bf16[2,512,2,128]{3,2,1,0:T(2,128)(2,1)}, s32[2]{0:T(128)S(1)}, s32[1024]{0:T(1024)S(1)}, bf16[1024,2,128]{0,2,1:T(8,128)(2,1)S(1)}...) while((s32[]{:T(128)}, ...), condition=%wide.region_6.7_spmd, body=%wide.region_3.6_spmd.sunk | while | flops 543949824 | bytes 12077299 | solution.py:66
  39.4 3.6 %fusion.89 = (f32[2,512]{1,0:T(2,128)S(1)}, bf16[2,512,1024]{2,1,0:T(8,128)(2,1)}) fusion(pred[512,1024]{1,0:T(8,128)(4,1)S(1)} %broadcast_compare_fusion.2, bf16[1024,2,128]{2,0,1:T(8,128)(2,1)S(1)} %get-tuple-element.196, bf16[1024,2,128]{0,2,1:T(8,128)(2,1)S(1)} %get-tuple-element.195, s32[]{:T(128)S(6)} %select_n.52), kind=kOutput, calls=%fused_computation.100.clone.1 | convolution fusion | flops 274727936 | bytes 3936260 | tf_op jit(solution)/shard_map/while/body/eval_jaxpr/sub | solution.py:56
  42.9 2.4 fusion.90
  48.2 3.6 %fusion.89 = (f32[2,512]{1,0:T(2,128)S(1)}, bf16[2,512,1024]{2,1,0:T(8,128)(2,1)}) fusion(pred[512,1024]{1,0:T(8,128)(4,1)S(1)} %broadcast_compare_fusion.2, bf16[1024,2,128]{2,0,1:T(8,128)(2,1)S(1)} %get-tuple-element.196, bf16[1024,2,128]{0,2,1:T(8,128)(2,1)S(1)} %get-tuple-element.195, s32[]{:T(128)S(6)} %select_n.52), kind=kOutput, calls=%fused_computation.100.clone.1 | convolution fusion | flops 274727936 | bytes 3936260 | tf_op jit(solution)/shard_map/while/body/eval_jaxpr/sub | solution.py:56
  51.8 2.4 fusion.90
  55.3 2.2 all_to_all.36
  57.4 4.9 %all-to-all-start.1 = ((bf16[8,128,256]{2,1,0:T(8,128)(2,1)}), bf16[8,128,256]{2,1,0:T(8,128)(2,1)S(1)}, u32[]{:S(2)}, u32[]{:S(2)}) async-start(bf16[8,128,256]{2,1,0:T(8,128)(2,1)} %all_to_all.36), calls=%async_computation.1 | async-start | bytes 1048576 | tf_op jit(solution)/shard_map/all_to_all | solution.py:175
  62.3 8.0 %convert_reduce_fusion = s32[1536,128]{1,0:T(8,128)S(1)} fusion(s32[128,8]{0,1:T(8,128)S(1)} %multiply_add_fusion), kind=kLoop, calls=%fused_computation.28 | loop fusion | flops 4521984 | bytes 790528 | tf_op jit(solution)/shard_map/reduce_sum | solution.py:189
  71.5 4.8 %multiply_reduce_fusion = (f32[128]{0:T(128)S(1)}, f32[128,2048]{1,0:T(8,128)S(1)}) fusion(bf16[128,2048]{0,1:T(8,128)(2,1)S(1)} %bitcast.100, bf16[2048,2048]{1,0:T(8,128)(2,1)} %param.26, bf16[128,2048]{1,0:T(8,128)(2,1)} %param.16), kind=kOutput, calls=%fused_computation.54 | convolution fusion | flops 1074790272 | bytes 10486272 | tf_op jit(solution)/shard_map/dot_general | solution.py:176
  76.3 4.5 %convolution_convert_fusion.2 = bf16[1536,2048]{1,0:T(8,128)(2,1)} fusion(f32[128,2048]{1,0:T(8,128)S(1)} %get-tuple-element.117, f32[2048]{0:T(1024)S(1)} %copy-done.7, f32[128]{0:T(128)S(1)} %add_rsqrt_fusion, s32[1536,128]{1,0:T(8,128)S(1)} %convert_reduce_fusion), kind=kOutput, calls=%fused_computation.27 | convolution fusion | flops 809435136 | bytes 8135168 | tf_op jit(solution)/shard_map/dot_general | solution.py:193
  80.8 11.0 %all-to-all-start.2 = ((bf16[64,24,2048]{2,1,0:T(8,128)(2,1)}), bf16[64,24,2048]{2,1,0:T(8,128)(2,1)}, u32[]{:S(2)}, u32[]{:S(2)}) async-start(bf16[64,24,2048]{2,1,0:T(8,128)(2,1)} %bitcast.93), calls=%async_computation.2 | async-start | bytes 12582912 | tf_op jit(solution)/shard_map/all_to_all | solution.py:71
  94.9 2.9 reduce
  97.9 4.0 %reshape.289 = bf16[16,2,32768]{2,1,0:T(2,128)(2,1)} reshape(bf16[16,65536]{1,0:T(8,128)(2,1)} %reduce) | data formatting | bytes 4194304
  101.9 71.9 %all-to-all-done.2 = bf16[64,24,2048]{2,1,0:T(8,128)(2,1)} async-done(((bf16[64,24,2048]{2,1,0:T(8,128)(2,1)}), bf16[64,24,2048]{2,1,0:T(8,128)(2,1)}, u32[]{:S(2)}, u32[]{:S(2)}) %all-to-all-start.2) | async-done | bytes 6291488 | tf_op jit(solution)/shard_map/all_to_all | solution.py:71
  173.8 9.7 %all-to-all-start.4 = ((bf16[16,2,32768]{2,1,0:T(2,128)(2,1)}), bf16[16,2,32768]{2,1,0:T(2,128)(2,1)S(1)}, u32[]{:S(2)}, u32[]{:S(2)}) async-start(bf16[16,2,32768]{2,1,0:T(2,128)(2,1)} %reshape.289), calls=%async_computation.4 | async-start | bytes 4194304 | tf_op jit(solution)/shard_map/all_to_all | solution.py:157
  183.5 10.0 %fusion.37 = f32[1536,1024]{1,0:T(8,128)S(1)} fusion(bf16[1536,2048]{1,0:T(8,128)(2,1)} %bitcast.15, bf16[1,2048,1024]{2,1,0:T(8,128)(2,1)} %param.28), kind=kOutput, calls=%fused_computation.34 | convolution fusion | flops 6442450944 | bytes 16777216 | tf_op jit(solution)/shard_map/dot_general | solution.py:81
  193.5 10.1 %fusion.35 = f32[1536,1024]{1,0:T(8,128)S(1)} fusion(bf16[1536,2048]{1,0:T(8,128)(2,1)} %bitcast.15, bf16[1,2048,1024]{2,1,0:T(8,128)(2,1)} %collective-permute-done), kind=kOutput, calls=%fused_computation.32 | convolution fusion | flops 6442450944 | bytes 16777216 | tf_op jit(solution)/shard_map/dot_general | solution.py:81
  203.7 6.4 %fusion.46 = f32[1536,2048]{1,0:T(8,128)} fusion(bf16[1,512,2048]{2,1,0:T(8,128)(2,1)S(1)} %copy-done.10, f32[1536,1024]{1,0:T(8,128)S(1)} %fusion.37), kind=kOutput, calls=%fused_computation.47 | convolution fusion | flops 3225944064 | bytes 20971520 | tf_op jit(solution)/shard_map/dot_general | solution.py:87
  210.1 8.8 %add_convert_fusion = bf16[1536,2048]{1,0:T(8,128)(2,1)} fusion(f32[1536,2048]{1,0:T(8,128)} %fusion.46, bf16[1,512,2048]{2,1,0:T(8,128)(2,1)} %collective-permute-done.1, f32[1536,1024]{1,0:T(8,128)S(1)} %fusion.35), kind=kOutput, calls=%fused_computation.26 | convolution fusion | flops 3232235520 | bytes 27262976 | tf_op jit(solution)/shard_map/dot_general | solution.py:88
  218.9 11.1 %all-to-all-start.3 = ((bf16[64,24,2048]{2,1,0:T(8,128)(2,1)}), bf16[64,24,2048]{2,1,0:T(8,128)(2,1)}, u32[]{:S(2)}, u32[]{:S(2)}) async-start(bf16[64,24,2048]{2,1,0:T(8,128)(2,1)} %bitcast.94), calls=%async_computation.3 | async-start | bytes 12582912 | tf_op jit(solution)/shard_map/all_to_all | solution.py:76
  230.8 2.9 select_reduce_fusion
  233.7 6.8 %reshape.290 = bf16[16,1,65536]{2,1,0:T(2,128)(2,1)} reshape(bf16[16,2,32768]{2,1,0:T(2,128)(2,1)S(1)} %all-to-all-done.4) | data formatting | bytes 4194304
  240.5 4.6 %convolution_convert_fusion.1 = bf16[8,65536]{1,0:T(8,128)(2,1)S(1)} fusion(bf16[16,1,65536]{2,1,0:T(2,128)(2,1)} %reshape.290, s32[8,16]{1,0:T(8,128)S(1)} %convert_reduce_fusion.2), kind=kOutput, calls=%fused_computation.25 | convolution fusion | flops 17301632 | bytes 3146240 | tf_op jit(solution)/shard_map/dot_general | solution.py:165
  246.3 64.6 %all-to-all-done.3 = bf16[64,24,2048]{2,1,0:T(8,128)(2,1)} async-done(((bf16[64,24,2048]{2,1,0:T(8,128)(2,1)}), bf16[64,24,2048]{2,1,0:T(8,128)(2,1)}, u32[]{:S(2)}, u32[]{:S(2)}) %all-to-all-start.3) | async-done | bytes 6291488 | tf_op jit(solution)/shard_map/all_to_all | solution.py:76
  311.0 3.8 %fusion.56 = f32[128,2048]{1,0:T(8,128)S(1)} fusion(bf16[1536,2048]{1,0:T(8,128)(2,1)} %bitcast.21, f32[128,1536]{1,0:T(8,128)S(1)} %copy-done), kind=kOutput, calls=%fused_computation.71 | convolution fusion | flops 805502976 | bytes 8126464 | tf_op jit(solution)/shard_map/dot_general | solution.py:209
  314.7 4.7 %fusion.42 = bf16[128,2048]{1,0:T(8,128)(2,1)} fusion(f32[128,2048]{1,0:T(8,128)S(1)} %get-tuple-element.117, f32[128,2048]{1,0:T(8,128)S(1)} %fusion.56, bf16[1536,2048]{1,0:T(8,128)(2,1)} %bitcast.21, f32[128,1536]{1,0:T(8,128)S(1)} %copy-done), kind=kOutput, calls=%fused_computation.43 | convolution fusion | flops 806879232 | bytes 9699328 | tf_op jit(solution)/shard_map/dot_general | solution.py:209
  (87 shorter events, 17.7 us)
Async XLA Ops:
  7.6 6.3 %copy-start.5 = (s32[128,8]{0,1:T(8,128)S(1)}, s32[128,8]{0,1:T(8,128)}, u32[]{:S(2)}) copy-start(s32[128,8]{0,1:T(8,128)} %param.24) | copy-start | bytes 12292
  9.0 24.9 %all-to-all-start = ((bf16[3,8,128,256]{2,3,0,1:T(8,128)(2,1)}), bf16[3,8,128,256]{2,3,0,1:T(8,128)(2,1)S(1)}, u32[]{:S(2)}, u32[]{:S(2)}) async-start(bf16[3,8,128,256]{2,3,0,1:T(8,128)(2,1)} %copy.97), calls=%async_computation | async-start | bytes 3145728 | tf_op jit(solution)/shard_map/all_to_all | solution.py:139
  35.2 2.3 copy-start.4
  42.9 2.4 copy-start.2
  45.6 0.8 copy-start.3
  51.8 2.4 copy-start.2
  54.5 0.8 copy-start.3
  57.4 13.8 %all-to-all-start.1 = ((bf16[8,128,256]{2,1,0:T(8,128)(2,1)}), bf16[8,128,256]{2,1,0:T(8,128)(2,1)S(1)}, u32[]{:S(2)}, u32[]{:S(2)}) async-start(bf16[8,128,256]{2,1,0:T(8,128)(2,1)} %all_to_all.36), calls=%async_computation.1 | async-start | bytes 1048576 | tf_op jit(solution)/shard_map/all_to_all | solution.py:175
  71.4 4.8 %copy-start.7 = (f32[2048]{0:T(1024)S(1)}, f32[2048]{0:T(1024)}, u32[]{:S(2)}) copy-start(f32[2048]{0:T(1024)} %param.27) | copy-start | bytes 24580
  80.8 11.6 %copy-start.6 = (s32[16,8]{0,1:T(8,128)S(1)}, s32[16,8]{0,1:T(8,128)}, u32[]{:S(2)}) copy-start(s32[16,8]{0,1:T(8,128)} %param.23) | copy-start | bytes 1540
  80.8 11.7 %copy-start.1 = (bf16[8,1,128,256]{2,3,0,1:T(8,128)(2,1)S(1)}, bf16[8,1,128,256]{2,3,0,1:T(8,128)(2,1)}, u32[]{:S(2)}) copy-start(bf16[8,1,128,256]{2,3,0,1:T(8,128)(2,1)} %get-tuple-element.104) | copy-start | bytes 1572868
  80.8 93.0 %all-to-all-start.2 = ((bf16[64,24,2048]{2,1,0:T(8,128)(2,1)}), bf16[64,24,2048]{2,1,0:T(8,128)(2,1)}, u32[]{:S(2)}, u32[]{:S(2)}) async-start(bf16[64,24,2048]{2,1,0:T(8,128)(2,1)} %bitcast.93), calls=%async_computation.2 | async-start | bytes 12582912 | tf_op jit(solution)/shard_map/all_to_all | solution.py:71
  91.8 101.8 %collective-permute-start = (bf16[1,2048,1024]{2,1,0:T(8,128)(2,1)}, bf16[1,2048,1024]{2,1,0:T(8,128)(2,1)}, u32[]{:S(2)}, u32[]{:S(2)}) collective-permute-start(bf16[1,2048,1024]{2,1,0:T(8,128)(2,1)} %param.28), channel_id=1, source_target_pairs={{0,1},{1,0},{2,3},{3,2},{4,5},{5,4},{6,7},{7,6},{8,9},{9,8},{10,11... | collective-permute-start | bytes 12582920 | tf_op jit(solution)/shard_map/ppermute | solution.py:19
  91.9 118.2 %collective-permute-start.1 = (bf16[1,512,2048]{2,1,0:T(8,128)(2,1)}, bf16[1,512,2048]{2,1,0:T(8,128)(2,1)}, u32[]{:S(2)}, u32[]{:S(2)}) collective-permute-start(bf16[1,512,2048]{2,1,0:T(8,128)(2,1)} %param.29), channel_id=1, source_target_pairs={{0,1},{1,0},{2,3},{3,2},{4,5},{5,4},{6,7},{7,6},{8,9},{9,8},{10,11... | collective-permute-start | bytes 6291464 | tf_op jit(solution)/shard_map/ppermute | solution.py:19
  173.8 45.2 %all-to-all-start.4 = ((bf16[16,2,32768]{2,1,0:T(2,128)(2,1)}), bf16[16,2,32768]{2,1,0:T(2,128)(2,1)S(1)}, u32[]{:S(2)}, u32[]{:S(2)}) async-start(bf16[16,2,32768]{2,1,0:T(2,128)(2,1)} %reshape.289), calls=%async_computation.4 | async-start | bytes 4194304 | tf_op jit(solution)/shard_map/all_to_all | solution.py:157
  193.5 10.2 %copy-start.10 = (bf16[1,512,2048]{2,1,0:T(8,128)(2,1)S(1)}, bf16[1,512,2048]{2,1,0:T(8,128)(2,1)}, u32[]{:S(2)}) copy-start(bf16[1,512,2048]{2,1,0:T(8,128)(2,1)} %param.29) | copy-start | bytes 6291460
  218.9 11.2 %copy-start.9 = (s32[16]{0:T(128)S(1)}, s32[16]{0:T(128)}, u32[]{:S(2)}) copy-start(s32[16]{0:T(128)} %param.22) | copy-start | bytes 196
  218.9 11.7 %copy-start.8 = (f32[128,8]{0,1:T(8,128)S(1)}, f32[128,8]{0,1:T(8,128)}, u32[]{:S(2)}) copy-start(f32[128,8]{0,1:T(8,128)} %param.25) | copy-start | bytes 12292
  218.9 92.0 %all-to-all-start.3 = ((bf16[64,24,2048]{2,1,0:T(8,128)(2,1)}), bf16[64,24,2048]{2,1,0:T(8,128)(2,1)}, u32[]{:S(2)}, u32[]{:S(2)}) async-start(bf16[64,24,2048]{2,1,0:T(8,128)(2,1)} %bitcast.94), calls=%async_computation.3 | async-start | bytes 12582912 | tf_op jit(solution)/shard_map/all_to_all | solution.py:76
  240.5 70.4 %copy-start = (f32[128,1536]{1,0:T(8,128)S(1)}, f32[128,1536]{1,0:T(8,128)}, u32[]{:S(2)}) copy-start(f32[128,1536]{1,0:T(8,128)} %select_reduce_fusion) | copy-start | bytes 2359300
